TPU v7x, 256 devices: a whole 4x4x8 slice. The times are simulated.
256 devices in a mesh: wide: 32 (over z, x), narrow: 8 (over y, core).
Axes of the slice: x: 4, y: 4, z: 8, core: 2. Of those that a mesh axis runs over, the one named last changes fastest.
Arguments:
- hidden_in: bfloat16 [64, 8192], P(None, 'wide'), may hold values from -6 to 6
- attn_gain: bfloat16 [8192], P('wide'), may hold values from 0.099609375 to 1.8984375
- qkv_weight: bfloat16 [8192, 8, 10, 128], P('wide', 'narrow'), may hold values from -2 to 2
- qkv_bias: bfloat16 [8, 10, 128], P('narrow'), may hold values from -3 to 3
- cache_keys: bfloat16 [64, 8, 4096, 128], P('wide', 'narrow'), may hold values from -256 to 256
- cache_values: bfloat16 [64, 8, 4096, 128], P('wide', 'narrow'), may hold values from -10 to 10
- positions: int32 [64, 3, 4096], P('wide'), may hold values from 0 to 4095
- lengths: int32 [64], P('wide'), may hold values from 512 to 4095, as said below
- out_weight: bfloat16 [8192, 8192], P('narrow', 'wide'), may hold values from -0.0625 to 0.0625
- mlp_gain: bfloat16 [8192], P('wide'), may hold values from 0.099609375 to 1.8984375
- gate_up_weight: bfloat16 [8192, 2, 29568], P('wide', None, 'narrow'), may hold values from -0.0625 to 0.0625
- down_weight: bfloat16 [29568, 8192], P('narrow', 'wide'), may hold values from -0.03125 to 0.03125
Outputs:
- layer_out: bfloat16 [64, 8192], P(None, 'wide')
Inputs may be any that keep to these rules, and one draw needn't show every extreme that they name: Slots 0 to lengths[b] - 1 of request b are filled, the new token takes slot lengths[b], and some request has 4095.
All inputs are finite; a program needn't handle non-finite values.
Results may differ from a plain program's by a relative error of at most 0.01115.
The roundings to bfloat16 on the way count: a program that leaves them out, or rounds other values in their place, can miss the bound.
Values may be sent and summed in bfloat16 or wider, within the bound.
No kernel may reach another device: no remote copies, remote signals or barrier semaphores. Data moves between devices by JAX's collectives and lax.ppermute only.
A program may use at most 64 MiB of HBM per device.

v0:
```python
import math
import jax
import jax.numpy as jnp
from jax import lax
from jax.sharding import PartitionSpec as P

D = 8192
DH = 128
CACHE = 4096
norm_eps = 1e-06
rope_base = 1000000.0


def mrope_tables(position):
    half_width = DH // 2
    pair_index = jnp.arange(half_width)
    inv_freq = jnp.exp(pair_index.astype(jnp.float32) * (-2.0 * math.log(rope_base) / DH))
    component = (pair_index >= DH // 8).astype(jnp.int32) + (
        pair_index >= DH // 8 + 3 * DH // 16
    ).astype(jnp.int32)
    pos_float = position.astype(jnp.float32)
    chosen = jnp.where(
        component == 0,
        pos_float[..., 0, :, None],
        jnp.where(component == 1, pos_float[..., 1, :, None], pos_float[..., 2, :, None]),
    )
    angles = chosen * inv_freq
    return (jnp.cos(angles), jnp.sin(angles))


def rotate(values, cosine, sine_table):
    half_width = values.shape[-1] // 2
    leading = values[..., :half_width]
    trailing = values[..., half_width:]
    return jnp.concatenate(
        [leading * cosine - trailing * sine_table, trailing * cosine + leading * sine_table],
        axis=-1,
    )


def local(
    hidden_in,
    attn_gain,
    qkv_weight,
    qkv_bias,
    cache_keys,
    cache_values,
    positions,
    lengths,
    out_weight,
    mlp_gain,
    gate_up_weight,
    down_weight,
):
    score_scale = 1.0 / math.sqrt(DH)
    owned = lengths.shape[0]
    local_rows = hidden_in.shape[1]
    kv_local = qkv_weight.shape[1]
    slot_count = qkv_weight.shape[2]
    group_size = slot_count - 2
    width = kv_local * slot_count * DH
    inputs = hidden_in.astype(jnp.float32)
    local_squares = jnp.sum(inputs * inputs, axis=1)
    scaled = (inputs * attn_gain.astype(jnp.float32)).astype(jnp.bfloat16)
    weight_flat = qkv_weight.reshape(local_rows, width)
    inv_rms = 1.0 / jnp.sqrt(lax.psum(local_squares, "wide") / D + norm_eps)
    row_block = scaled
    factor = inv_rms
    projected = lax.psum_scatter(
        factor[:, None] * jnp.dot(row_block, weight_flat, preferred_element_type=jnp.float32),
        "wide",
        scatter_dimension=0,
        tiled=True,
    )
    projected = projected + qkv_bias.reshape(width).astype(jnp.float32)
    projected = projected.reshape(owned, kv_local, slot_count, DH)
    cosine, sine_table = mrope_tables(positions)
    keys_rot = rotate(cache_keys.astype(jnp.float32), cosine[:, None], sine_table[:, None]).astype(
        jnp.bfloat16
    )
    new_position = jnp.take_along_axis(positions, lengths[:, None, None], axis=2)
    cos_new, sin_new = mrope_tables(new_position)
    query = rotate(projected[:, :, :group_size], cos_new[:, None], sin_new[:, None]).astype(
        jnp.bfloat16
    )
    key_new = rotate(projected[:, :, group_size], cos_new, sin_new).astype(jnp.bfloat16)
    value_new = projected[:, :, group_size + 1].astype(jnp.bfloat16)
    scores = (
        jnp.einsum("rgjd,rgsd->rgjs", query, keys_rot, preferred_element_type=jnp.float32)
        * score_scale
    )
    own_score = (
        jnp.sum(query.astype(jnp.float32) * key_new.astype(jnp.float32)[:, :, None, :], axis=3)
        * score_scale
    )
    valid_slot = jnp.arange(CACHE)[None, None, None, :] < lengths[:, None, None, None]
    row_max = jnp.maximum(jnp.max(jnp.where(valid_slot, scores, -jnp.inf), axis=3), own_score)
    probabilities = jnp.where(valid_slot, jnp.exp(scores - row_max[..., None]), 0.0)
    own_prob = jnp.exp(own_score - row_max)
    totals = jnp.sum(probabilities, axis=3) + own_prob
    probs_rounded = probabilities.astype(jnp.bfloat16)
    own_rounded = own_prob.astype(jnp.bfloat16).astype(jnp.float32)
    weighted = jnp.einsum(
        "rgjs,rgsd->rgjd", probs_rounded, cache_values, preferred_element_type=jnp.float32
    )
    weighted = weighted + own_rounded[..., None] * value_new.astype(jnp.float32)[:, :, None, :]
    attended = (
        (weighted / totals[..., None])
        .astype(jnp.bfloat16)
        .reshape(owned, kv_local * group_size * DH)
    )
    head_partial = jnp.dot(
        lax.all_gather(attended, "wide", axis=0, tiled=True),
        out_weight,
        preferred_element_type=jnp.float32,
    )
    attn_out = lax.psum(head_partial, "narrow")
    residual = (inputs + attn_out).astype(jnp.bfloat16)
    resid_float = residual.astype(jnp.float32)
    resid_squares = jnp.sum(resid_float * resid_float, axis=1)
    scaled2 = (resid_float * mlp_gain.astype(jnp.float32)).astype(jnp.bfloat16)
    hidden_local = gate_up_weight.shape[2]
    gate_up_flat = gate_up_weight.reshape(local_rows, 2 * hidden_local)
    inv_rms2 = 1.0 / jnp.sqrt(lax.psum(resid_squares, "wide") / D + norm_eps)
    row_block = scaled2
    factor = inv_rms2
    gate_up = lax.psum_scatter(
        factor[:, None] * jnp.dot(row_block, gate_up_flat, preferred_element_type=jnp.float32),
        "wide",
        scatter_dimension=0,
        tiled=True,
    )
    hidden = (jax.nn.silu(gate_up[:, :hidden_local]) * gate_up[:, hidden_local:]).astype(
        jnp.bfloat16
    )
    down_partial = jnp.dot(
        lax.all_gather(hidden, "wide", axis=0, tiled=True),
        down_weight,
        preferred_element_type=jnp.float32,
    )
    mlp_out = lax.psum(down_partial, "narrow")
    return (resid_float + mlp_out).astype(jnp.bfloat16)


def solution(mesh):
    in_specs = (
        P(None, "wide"),
        P("wide"),
        P("wide", "narrow", None, None),
        P("narrow", None, None),
        P("wide", "narrow", None, None),
        P("wide", "narrow", None, None),
        P("wide", None, None),
        P("wide"),
        P("narrow", "wide"),
        P("wide"),
        P("wide", None, "narrow"),
        P("narrow", "wide"),
    )
    out_specs = P(None, "wide")
    return jax.shard_map(local, mesh=mesh, in_specs=in_specs, out_specs=out_specs, check_vma=False)
```

profile of v0, /device:TPU:2, one launch (start us, length us, event | category | flops | bytes accessed | tf_op | source)
XLA Modules:
  0.0 691.7 jit_solution(1203411043637431055)
XLA Ops:
  6.5 1.5 copy.20
  8.0 0.9 fusion.24
  8.9 73.7 %psum.28 = f32[64]{0:T(128)S(1)} all-reduce(f32[64]{0:T(128)S(1)} %fusion.24), channel_id=1, replica_groups=mesh['wide'=32,'narrow'=8] {'wide'}, use_global_device_ids=true, to_apply=%region_1.0 | all-reduce | flops 64 | bytes 512 | tf_op jit(solution)/shard_map/psum | solution.py:66
  83.3 1.8 convolution_multiply_fusion.2
  85.2 0.9 convert_element_type.179
  86.1 3.4 copy.22
  89.7 3.8 bitcast_convert_fusion
  93.8 1.4 gather_fusion
  95.6 19.8 %fusion.7 = (bf16[2,4096,64]{2,1,0:T(8,128)(2,1)}, bf16[2,4096,64]{2,1,0:T(8,128)(2,1)}) fusion(f32[2,1,4096,128]{3,2,0,1:T(8,128)} %bitcast_convert_fusion, f32[64]{0:T(128)S(1)} %multiply_exponential_fusion, f32[2,4096]{1,0:T(2,128)S(1)} %get-tuple-element.17, f32[2,4096]{1,0:T(2,128)S(1)} %get-tuple-element.18, f32[2,4096]{1,0:T(2,128)S(1)} %get-tuple-element.16, ...), kind=kLoop, calls=%fused_computation.15 | loop fusion | flops 5767168 | bytes 6390144 | tf_op jit(solution)/shard_map/concatenate | solution.py:35
  116.8 112.9 %all-reduce.11.cloned.1.call-done = f32[64,1280]{1,0:T(8,128)} async-done(((f32[64,1280]{1,0:T(8,128)}), f32[64,1280]{1,0:T(8,128)}) %all-reduce.11.cloned.1.call-update) | async-done | bytes 327696
  229.7 0.8 dynamic-slice_add_fusion
  231.0 3.6 select_reduce_fusion
  235.3 41.5 %all-gather = bf16[32,2,1024]{2,1,0:T(2,128)(2,1)S(1)} all-gather(bf16[1,2,1024]{2,1,0:T(2,128)(2,1)S(1)} %reshape.655), channel_id=1, replica_groups=mesh['wide'=32,'narrow'=8] {'wide'}, dimensions={0}, use_global_device_ids=true | all-gather | bytes 135168 | tf_op jit(solution)/shard_map/all_gather | solution.py:113
  276.9 0.8 fusion.52
  277.8 63.5 %all-reduce.7.cloned.1.call-done = f32[64,256]{1,0:T(8,128)} async-done(((f32[64,256]{1,0:T(8,128)}), f32[64,256]{1,0:T(8,128)}) %all-reduce.7.cloned.1.call-update) | async-done | bytes 65552 | tf_op jit(solution)/shard_map/psum | solution.py:117
  341.3 0.9 fusion.27
  342.3 71.1 %psum.30 = f32[64]{0:T(128)S(1)} all-reduce(f32[64]{0:T(128)S(1)} %get-tuple-element.8), channel_id=1, replica_groups=mesh['wide'=32,'narrow'=8] {'wide'}, use_global_device_ids=true, to_apply=%region_8.9 | all-reduce | flops 64 | bytes 512 | tf_op jit(solution)/shard_map/psum | solution.py:124
  413.4 4.6 convolution_multiply_fusion
  418.1 149.5 %all-reduce.13.cloned.1.call-done = f32[64,7392]{1,0:T(8,128)} async-done(((f32[64,7392]{1,0:T(8,128)}), f32[64,7392]{1,0:T(8,128)}) %all-reduce.13.cloned.1.call-update) | async-done | bytes 1892368
  567.6 1.1 fusion.36
  568.7 48.7 %all-gather.1 = bf16[32,2,3696]{2,1,0:T(2,128)(2,1)S(1)} all-gather(bf16[1,2,3696]{2,1,0:T(2,128)(2,1)S(1)} %fusion.36), channel_id=1, replica_groups=mesh['wide'=32,'narrow'=8] {'wide'}, dimensions={0}, use_global_device_ids=true | all-gather | bytes 487872 | tf_op jit(solution)/shard_map/all_gather | solution.py:137
  617.7 2.6 fusion.53
  620.3 63.4 %all-reduce.9.cloned.1.call-done = f32[64,256]{1,0:T(8,128)} async-done(((f32[64,256]{1,0:T(8,128)}), f32[64,256]{1,0:T(8,128)}) %all-reduce.9.cloned.1.call-update) | async-done | bytes 65552 | tf_op jit(solution)/shard_map/psum | solution.py:141
  683.7 1.5 fusion.29
  (57 shorter events, 4.0 us)
Async XLA Ops:
  6.5 228.3 %copy-start = (bf16[2,1,4096,128]{3,2,1,0:T(8,128)(2,1)S(1)}, bf16[2,1,4096,128]{3,2,1,0:T(8,128)(2,1)}, u32[]{:S(2)}) copy-start(bf16[2,1,4096,128]{3,2,1,0:T(8,128)(2,1)} %param.17) | copy-start | bytes 6291460
  6.5 83.0 %copy-start.4 = (s32[2]{0:T(128)S(1)}, s32[2]{0:T(128)}, u32[]{:S(2)}) copy-start(s32[2]{0:T(128)} %param.19) | copy-start | bytes 28
  6.5 223.2 %all-reduce.11.cloned.1.call-start = ((), (), s32[]{:S(2)}) async-start(), calls=%async_computation.2 | async-start | bytes 655360
  85.1 256.2 %all-reduce.7.cloned.1.call-start = ((), (), s32[]{:S(2)}) async-start(), calls=%async_computation | async-start | bytes 131072 | tf_op jit(solution)/shard_map/psum | solution.py:117
  95.6 20.0 %copy-start.6 = (u32[256]{0:T(256)S(1)}, u32[256]{0:T(256)}, u32[]{:S(2)}) copy-start(u32[256]{0:T(256)} %constant.61) | copy-start | bytes 3076
  95.6 21.2 %copy-start.3 = (bf16[1,10,128]{2,1,0:T(8,128)(2,1)S(1)}, bf16[1,10,128]{2,1,0:T(8,128)(2,1)}, u32[]{:S(2)}) copy-start(bf16[1,10,128]{2,1,0:T(8,128)(2,1)} %param.15) | copy-start | bytes 7684
  231.0 45.9 %copy-start.1 = (bf16[1024,256]{1,0:T(8,128)(2,1)S(1)}, bf16[1024,256]{1,0:T(8,128)(2,1)}, u32[]{:S(2)}) copy-start(bf16[1024,256]{1,0:T(8,128)(2,1)} %param.20) | copy-start | bytes 1572868
  231.0 46.8 %copy-start.5 = (bf16[256]{0:T(256)(128)(2,1)S(1)}, bf16[256]{0:T(256)(128)(2,1)}, u32[]{:S(2)}) copy-start(bf16[256]{0:T(256)(128)(2,1)} %param.21) | copy-start | bytes 1540
  231.0 110.4 %copy-start.2 = (bf16[64,256]{1,0:T(8,128)(2,1)S(1)}, bf16[64,256]{1,0:T(8,128)(2,1)}, u32[]{:S(2)}) copy-start(bf16[64,256]{1,0:T(8,128)(2,1)} %param.12) | copy-start | bytes 98308
  277.7 289.9 %all-reduce.13.cloned.1.call-start = ((), (), s32[]{:S(2)}) async-start(), calls=%async_computation.3 | async-start | bytes 3801088
  418.0 265.6 %all-reduce.9.cloned.1.call-start = ((), (), s32[]{:S(2)}) async-start(), calls=%async_computation.1 | async-start | bytes 131072 | tf_op jit(solution)/shard_map/psum | solution.py:141
Sparse Core Ops, SparseCore 0:
  85.3 144.4 all-reduce.10
  277.9 63.4 all-reduce.6
  418.2 149.3 all-reduce.12
  620.4 63.1 all-reduce.8
where the time goes:
time: 692 us
  waiting for transfers between devices  389 us (56%)
  blocking collectives  235 us (34%)
  other arithmetic  31.6 us (5%)
  between operations  14 us (2%)
  matrix products  13.9 us (2%)
  local copies, waits for them, and re-layouts  7.72 us (1%)
    unnamed x6, waiting for transfers between devices  262 us
    psum x1, blocking collectives, local(): inv_rms = 1.0 / jnp.sqrt(lax.psum(local_squares, 'wide') / D + norm_eps)  73.7 us
    psum x1, blocking collectives, local(): inv_rms2 = 1.0 / jnp.sqrt(lax.psum(resid_squares, 'wide') / D + norm_eps)  71.1 us
    psum x1, waiting for transfers between devices, local(): attn_out = lax.psum(head_partial, 'narrow')  63.5 us
    psum x1, waiting for transfers between devices, local(): mlp_out = lax.psum(down_partial, 'narrow')  63.4 us
    all_gather x1, blocking collectives, local(): lax.all_gather(hidden, 'wide', axis=0, tiled=True)  48.7 us
    all_gather x1, blocking collectives, local(): lax.all_gather(attended, 'wide', axis=0, tiled=True)  41.5 us
    concatenate x2, other arithmetic, rotate(): jnp.concatenate([leading * cosine - trailing * sine_table, trailing * cos...  19.8 us
  transfers between devices with their start and end apart: 4, of which 4 were waited for; matrix products, arithmetic and copies ran while one was open for 4% of the time, Pallas kernels for 0%

commit v1 on v0

--- a/solution.py
+++ b/solution.py
@@ -3,6 +3,7 @@
 import jax.numpy as jnp
 from jax import lax
 from jax.sharding import PartitionSpec as P
+from jax.lax import axis_size, ppermute
 
 D = 8192
 DH = 128
@@ -138,7 +139,10 @@
         down_weight,
         preferred_element_type=jnp.float32,
     )
-    mlp_out = lax.psum(down_partial, "narrow")
+    lanes = axis_size("narrow")
+    mlp_out = down_partial
+    for dd in [[(s, s ^ at) for s in range(lanes)] for at in (1, 2, 4, 8, 16) if at < lanes]:
+        mlp_out = mlp_out + ppermute(mlp_out, "narrow", dd)
     return (resid_float + mlp_out).astype(jnp.bfloat16)
 
 

time: 692 us -> 640 us (0.925)
  waiting for transfers between devices: 389 us -> 333 us
    psum x1 -> x0, waiting for transfers between devices: 63.4 us -> none  [local(): mlp_out = lax.psum(down_partial, 'narrow')]
    unnamed x6 -> x5, waiting for transfers between devices: 262 us -> 262 us
  transfers between devices with their start and end apart: 4 -> 6, of which waited for: 4 -> 6; matrix products, arithmetic and copies ran while one was open for 4% -> 5% of each run, Pallas kernels for 0% -> 0%
where the time goes in v1:
time: 640 us; the launch traced here: 638 us
  waiting for transfers between devices  333 us (52%)
  blocking collectives  235 us (37%)
  other arithmetic  30.8 us (5%)
  between operations  14 us (2%)
  matrix products  13.3 us (2%)
  local copies, waits for them, and re-layouts  7.72 us (1%)
    unnamed x5, waiting for transfers between devices  262 us
    psum x1, blocking collectives, local(): inv_rms = 1.0 / jnp.sqrt(lax.psum(local_squares, 'wide') / D + norm_eps)  73.7 us
    psum x1, blocking collectives, local(): inv_rms2 = 1.0 / jnp.sqrt(lax.psum(resid_squares, 'wide') / D + norm_eps)  71.1 us
    psum x1, waiting for transfers between devices, local(): attn_out = lax.psum(head_partial, 'narrow')  63.5 us
    all_gather x1, blocking collectives, local(): lax.all_gather(hidden, 'wide', axis=0, tiled=True)  48.7 us
    all_gather x1, blocking collectives, local(): lax.all_gather(attended, 'wide', axis=0, tiled=True)  41.5 us
    concatenate x2, other arithmetic, rotate(): jnp.concatenate([leading * cosine - trailing * sine_table, trailing * cos...  19.8 us
  transfers between devices with their start and end apart: 6, of which 6 were waited for; matrix products, arithmetic and copies ran while one was open for 5% of the time, Pallas kernels for 0%

profile of v1, /device:TPU:2, one launch (start us, length us, event | category | flops | bytes accessed | tf_op | source)
XLA Modules:
  0.0 638.4 jit_solution(13457229106401969257)
XLA Ops:
  6.5 1.5 copy.20
  8.9 73.7 %psum.21 = f32[64]{0:T(128)S(1)} all-reduce(f32[64]{0:T(128)S(1)} %fusion.24), channel_id=1, replica_groups=mesh['wide'=32,'narrow'=8] {'wide'}, use_global_device_ids=true, to_apply=%region_1.0 | all-reduce | flops 64 | bytes 512 | tf_op jit(solution)/shard_map/psum | solution.py:67
  83.3 1.8 convolution_multiply_fusion.2
  85.2 0.9 convert_element_type.179
  86.1 3.4 copy.22
  89.7 3.8 bitcast_convert_fusion
  93.8 1.4 gather_fusion
  95.6 19.8 %fusion.7 = (bf16[2,4096,64]{2,1,0:T(8,128)(2,1)}, bf16[2,4096,64]{2,1,0:T(8,128)(2,1)}) fusion(f32[2,1,4096,128]{3,2,0,1:T(8,128)} %bitcast_convert_fusion, f32[64]{0:T(128)S(1)} %multiply_exponential_fusion, f32[2,4096]{1,0:T(2,128)S(1)} %get-tuple-element.17, f32[2,4096]{1,0:T(2,128)S(1)} %get-tuple-element.18, f32[2,4096]{1,0:T(2,128)S(1)} %get-tuple-element.16, ...), kind=kLoop, calls=%fused_computation.15 | loop fusion | flops 5767168 | bytes 6390144 | tf_op jit(solution)/shard_map/concatenate | solution.py:36
  116.8 112.9 %all-reduce.8.cloned.1.call-done = f32[64,1280]{1,0:T(8,128)} async-done(((f32[64,1280]{1,0:T(8,128)}), f32[64,1280]{1,0:T(8,128)}) %all-reduce.8.cloned.1.call-update) | async-done | bytes 327696
  231.0 3.6 select_reduce_fusion
  235.3 41.5 %all-gather = bf16[32,2,1024]{2,1,0:T(2,128)(2,1)S(1)} all-gather(bf16[1,2,1024]{2,1,0:T(2,128)(2,1)S(1)} %reshape.655), channel_id=1, replica_groups=mesh['wide'=32,'narrow'=8] {'wide'}, dimensions={0}, use_global_device_ids=true | all-gather | bytes 135168 | tf_op jit(solution)/shard_map/all_gather | solution.py:114
  277.8 63.5 %all-reduce.6.cloned.1.call-done = f32[64,256]{1,0:T(8,128)} async-done(((f32[64,256]{1,0:T(8,128)}), f32[64,256]{1,0:T(8,128)}) %all-reduce.6.cloned.1.call-update) | async-done | bytes 65552 | tf_op jit(solution)/shard_map/psum | solution.py:118
  341.3 0.9 fusion.27
  342.3 71.1 %psum.23 = f32[64]{0:T(128)S(1)} all-reduce(f32[64]{0:T(128)S(1)} %get-tuple-element.8), channel_id=1, replica_groups=mesh['wide'=32,'narrow'=8] {'wide'}, use_global_device_ids=true, to_apply=%region_8.9 | all-reduce | flops 64 | bytes 512 | tf_op jit(solution)/shard_map/psum | solution.py:125
  413.4 4.6 convolution_multiply_fusion
  418.0 149.5 %all-reduce.10.cloned.1.call-done = f32[64,7392]{1,0:T(8,128)} async-done(((f32[64,7392]{1,0:T(8,128)}), f32[64,7392]{1,0:T(8,128)}) %all-reduce.10.cloned.1.call-update) | async-done | bytes 1892368
  567.6 1.1 fusion.36
  568.7 48.7 %all-gather.1 = bf16[32,2,3696]{2,1,0:T(2,128)(2,1)S(1)} all-gather(bf16[1,2,3696]{2,1,0:T(2,128)(2,1)S(1)} %fusion.36), channel_id=1, replica_groups=mesh['wide'=32,'narrow'=8] {'wide'}, dimensions={0}, use_global_device_ids=true | all-gather | bytes 487872 | tf_op jit(solution)/shard_map/all_gather | solution.py:138
  617.7 2.0 fusion.53
  619.8 1.2 collective-permute-done
  621.0 1.6 collective-permute-start.1
  622.6 2.8 collective-permute-done.1
  625.4 3.1 collective-permute-start.2
  628.5 2.8 collective-permute-done.2
  (62 shorter events, 7.1 us)
Async XLA Ops:
  6.5 228.3 %copy-start = (bf16[2,1,4096,128]{3,2,1,0:T(8,128)(2,1)S(1)}, bf16[2,1,4096,128]{3,2,1,0:T(8,128)(2,1)}, u32[]{:S(2)}) copy-start(bf16[2,1,4096,128]{3,2,1,0:T(8,128)(2,1)} %param.17) | copy-start | bytes 6291460
  6.5 83.0 %copy-start.4 = (s32[2]{0:T(128)S(1)}, s32[2]{0:T(128)}, u32[]{:S(2)}) copy-start(s32[2]{0:T(128)} %param.19) | copy-start | bytes 28
  6.5 223.2 %all-reduce.8.cloned.1.call-start = ((), (), s32[]{:S(2)}) async-start(), calls=%async_computation.1 | async-start | bytes 655360
  85.1 256.2 %all-reduce.6.cloned.1.call-start = ((), (), s32[]{:S(2)}) async-start(), calls=%async_computation | async-start | bytes 131072 | tf_op jit(solution)/shard_map/psum | solution.py:118
  95.6 20.0 %copy-start.6 = (u32[256]{0:T(256)S(1)}, u32[256]{0:T(256)}, u32[]{:S(2)}) copy-start(u32[256]{0:T(256)} %constant.61) | copy-start | bytes 3076
  95.6 21.2 %copy-start.3 = (bf16[1,10,128]{2,1,0:T(8,128)(2,1)S(1)}, bf16[1,10,128]{2,1,0:T(8,128)(2,1)}, u32[]{:S(2)}) copy-start(bf16[1,10,128]{2,1,0:T(8,128)(2,1)} %param.15) | copy-start | bytes 7684
  231.0 45.9 %copy-start.1 = (bf16[1024,256]{1,0:T(8,128)(2,1)S(1)}, bf16[1024,256]{1,0:T(8,128)(2,1)}, u32[]{:S(2)}) copy-start(bf16[1024,256]{1,0:T(8,128)(2,1)} %param.20) | copy-start | bytes 1572868
  231.0 46.8 %copy-start.5 = (bf16[256]{0:T(256)(128)(2,1)S(1)}, bf16[256]{0:T(256)(128)(2,1)}, u32[]{:S(2)}) copy-start(bf16[256]{0:T(256)(128)(2,1)} %param.21) | copy-start | bytes 1540
  231.0 110.4 %copy-start.2 = (bf16[64,256]{1,0:T(8,128)(2,1)S(1)}, bf16[64,256]{1,0:T(8,128)(2,1)}, u32[]{:S(2)}) copy-start(bf16[64,256]{1,0:T(8,128)(2,1)} %param.12) | copy-start | bytes 98308
  277.7 289.9 %all-reduce.10.cloned.1.call-start = ((), (), s32[]{:S(2)}) async-start(), calls=%async_computation.2 | async-start | bytes 3801088
  619.7 1.3 collective-permute-start
  621.0 4.4 collective-permute-start.1
  625.4 5.9 collective-permute-start.2
Sparse Core Ops, SparseCore 0:
  85.3 144.4 all-reduce.7
  277.9 63.4 all-reduce.5
  418.2 149.3 all-reduce.9
